TPU v7x, 256 devices: a whole 4x4x8 slice. The times are simulated.
256 devices in a mesh: row: 8 (over y, core), col: 32 (over x, z).
Axes of the slice: x: 4, y: 4, z: 8, core: 2. Of those that a mesh axis runs over, the one named last changes fastest.
Arguments:
- hidden: bfloat16 [32768, 4608], P('col', 'row'), may hold values from -6 to 6
- w_query: bfloat16 [4608, 4096], P('col', 'row'), may hold values from -0.09375 to 0.09375
- w_key: bfloat16 [4608, 2048], P('col', 'row'), may hold values from -0.09375 to 0.09375
- w_value: bfloat16 [4608, 2048], P('col', 'row'), may hold values from -0.09375 to 0.09375
- adapter_down: bfloat16 [32, 4608, 32], P('col', 'row'), may hold values from -0.09375 to 0.09375
- adapter_up_query: bfloat16 [32, 16, 4096], P('col', None, 'row'), may hold values from -1.5 to 1.5
- adapter_up_value: bfloat16 [32, 16, 2048], P('col', None, 'row'), may hold values from -1.5 to 1.5
- lengths: int32 [32, 10], P('col'), may hold values from 1 to 192, 1024 in all within a row
- request_adapter: int32 [32, 10], P('col'), may hold values from 0 to 31
- adapter_slot: int32 [32], replicated, may hold values from 0 to 31, each once
- page_table: int32 [32, 18], P('col'), may hold values from 0 to 17, each once within a row
Outputs:
- query: bfloat16 [32768, 4096], P('col', 'row')
- key_cache: bfloat16 [576, 128, 2048], P('col', None, 'row')
- value_cache: bfloat16 [576, 128, 2048], P('col', None, 'row')
Inputs may be any that keep to these rules, and one draw needn't show every extreme that they name: Each row of lengths sums to 1024, and its longest request has exactly 192 tokens. `adapter_slot`: a permutation of the slots. `page_table`: each row is a permutation of the 18 local slots.
All inputs are finite; a program needn't handle non-finite values.
Results may differ from a plain program's by a relative error of at most 0.0039.
Values may be sent and summed in bfloat16 or wider, within the bound.
No kernel may reach another device: no remote copies, remote signals or barrier semaphores. Data moves between devices by JAX's collectives and lax.ppermute only.
A program may use at most 128 MiB of HBM per device.

v0:
```python
import math
import jax
import jax.numpy as jnp
from jax import lax
from jax.sharding import PartitionSpec as P

HEAD = 128
PAGE = 128
MOST = 192
TOK_DEV = 1024


def rotate(values, position):
    half_width = HEAD // 2
    frequency = jnp.exp(
        jnp.arange(half_width, dtype=jnp.float32) * (-2.0 * math.log(10000.0) / HEAD)
    )
    angles = position.astype(jnp.float32)[:, None] * frequency[None, :]
    cosine = jnp.cos(angles)[:, None, :]
    sine_value = jnp.sin(angles)[:, None, :]
    shaped = values.reshape(values.shape[0], -1, HEAD)
    leading = shaped[:, :, :half_width]
    second = shaped[:, :, half_width:]
    rotated = jnp.concatenate(
        [leading * cosine - second * sine_value, second * cosine + leading * sine_value], axis=2
    )
    return rotated.reshape(values.shape)


def layout(lengths, page_row):
    token_index = jnp.arange(TOK_DEV, dtype=jnp.int32)
    starts = jnp.cumsum(lengths) - lengths
    request_of = jnp.sum((token_index[:, None] >= starts[None, :]).astype(jnp.int32), axis=1) - 1
    position = token_index - jnp.take(starts, request_of)
    pages_each = (lengths + PAGE - 1) // PAGE
    page_start = jnp.cumsum(pages_each) - pages_each
    page_index = jnp.take(page_start, request_of) + position // PAGE
    target = jnp.take(page_row, page_index) * PAGE + position % PAGE
    return (starts, request_of, position, target)


def expand_up(lowrank, chosen, up_query, up_value):
    adapter_count = up_query.shape[0]
    rank_width = up_query.shape[1]
    onehot = (chosen[:, None] == jnp.arange(adapter_count, dtype=jnp.int32)[None, :]).astype(
        lowrank.dtype
    )
    spread_query = (onehot[:, :, None] * lowrank[:, None, :rank_width]).reshape(
        -1, adapter_count * rank_width
    )
    spread_value = (onehot[:, :, None] * lowrank[:, None, rank_width:]).reshape(
        -1, adapter_count * rank_width
    )
    delta_query = jnp.dot(
        spread_query,
        up_query.reshape(adapter_count * rank_width, -1),
        preferred_element_type=jnp.float32,
    )
    delta_value = jnp.dot(
        spread_value,
        up_value.reshape(adapter_count * rank_width, -1),
        preferred_element_type=jnp.float32,
    )
    return (delta_query, delta_value)


def project_down(source, down_all, starts, lengths, chosen_request):
    tokens = source.shape[0]
    padded = jnp.concatenate([source, jnp.zeros((MOST, source.shape[1]), source.dtype)], axis=0)
    result = jnp.zeros((tokens + MOST, down_all.shape[2]), jnp.float32)
    inner_rows = jnp.arange(MOST, dtype=jnp.int32)

    def one_request(number, result):
        first_row = starts[number]
        window = lax.dynamic_slice_in_dim(padded, first_row, MOST, 0)
        factor = lax.dynamic_index_in_dim(down_all, chosen_request[number], 0, keepdims=False)
        partial_sum = jnp.dot(window, factor, preferred_element_type=jnp.float32)
        inside = (inner_rows < lengths[number]).astype(jnp.float32)[:, None]
        current = lax.dynamic_slice_in_dim(result, first_row, MOST, 0)
        return lax.dynamic_update_slice_in_dim(result, current + partial_sum * inside, first_row, 0)

    result = lax.fori_loop(0, starts.shape[0], one_request, result)
    return result[:tokens]


def shards(
    hidden,
    w_query,
    w_key,
    w_value,
    adapter_down,
    adapter_up_query,
    adapter_up_value,
    lengths,
    request_adapter,
    adapter_slot,
    page_table,
):
    starts, request_of, position, target = layout(lengths[0], page_table[0])
    full_rows = lax.all_gather(hidden, "row", axis=1, tiled=True)
    base_query = jnp.dot(
        full_rows,
        lax.all_gather(w_query, "col", axis=0, tiled=True),
        preferred_element_type=jnp.float32,
    )
    base_key = jnp.dot(
        full_rows,
        lax.all_gather(w_key, "col", axis=0, tiled=True),
        preferred_element_type=jnp.float32,
    )
    base_value = jnp.dot(
        full_rows,
        lax.all_gather(w_value, "col", axis=0, tiled=True),
        preferred_element_type=jnp.float32,
    )
    up_query, up_value = (
        lax.all_gather(adapter_up_query, "col", axis=0, tiled=True),
        lax.all_gather(adapter_up_value, "col", axis=0, tiled=True),
    )
    chosen_request = jnp.take(adapter_slot, request_adapter[0])
    rows_all = lax.all_gather(adapter_down, "row", axis=1, tiled=True)
    down_all = lax.all_gather(rows_all, "col", axis=0, tiled=True)
    lowrank = project_down(full_rows, down_all, starts, lengths[0], chosen_request)
    lowrank = lowrank.astype(jnp.bfloat16)
    chosen = jnp.take(chosen_request, request_of)
    delta_query, delta_value = expand_up(lowrank, chosen, up_query, up_value)
    query = rotate(base_query + delta_query, position).astype(jnp.bfloat16)
    key_rotated = rotate(base_key, position).astype(jnp.bfloat16)
    value_rows = (base_value + delta_value).astype(jnp.bfloat16)
    pages = page_table.shape[1]
    key_width = w_key.shape[1]
    key_cache = (
        jnp.zeros((pages * PAGE, key_width), jnp.bfloat16)
        .at[target]
        .set(key_rotated)
        .reshape(pages, PAGE, key_width)
    )
    value_cache = (
        jnp.zeros((pages * PAGE, key_width), jnp.bfloat16)
        .at[target]
        .set(value_rows)
        .reshape(pages, PAGE, key_width)
    )
    return (query, key_cache, value_cache)


def solution(mesh):
    return jax.shard_map(
        shards,
        mesh=mesh,
        in_specs=(
            P("col", "row"),
            P("col", "row"),
            P("col", "row"),
            P("col", "row"),
            P("col", "row", None),
            P("col", None, "row"),
            P("col", None, "row"),
            P("col", None),
            P("col", None),
            P(),
            P("col", None),
        ),
        out_specs=(P("col", "row"), P("col", None, "row"), P("col", None, "row")),
        check_vma=False,
    )
```

profile of v0, /device:TPU:1, one launch (start us, length us, event | category | flops | bytes accessed | tf_op | source)
XLA Modules:
  0.0 450.9 jit_solution(18159563451350654746)
XLA Ops:
  9.4 1.0 copy.40
  10.4 18.8 %all_gather.26 = bf16[1,4608,32]{2,0,1:T(2,128)(2,1)S(1)} all-gather(bf16[1,576,32]{2,0,1:T(2,128)(2,1)S(1)} %copy.40), channel_id=1, replica_groups=mesh['row'=8,'col'=32] {'row'}, dimensions={1}, use_global_device_ids=true | all-gather | bytes 331776 | tf_op jit(solution)/shard_map/all_gather | solution.py:121
  29.3 3.7 copy.41
  33.6 0.7 fusion.36
  37.6 24.0 %compare_select_fusion.1 = (s32[1024]{0:T(1024)S(1)}, pred[1024]{0:T(1024)(128)(4,1)S(1)}, pred[1024]{0:T(1024)(128)(4,1)S(1)}, pred[1024]{0:T(1024)(128)(4,1)S(...) fusion(s32[]{:T(128)} %bitcast.41, s32[]{:T(128)} %bitcast.40, ...), kind=kLoop, calls=%fused_computation.41 | loop fusion | flops 105472 | bytes 18584 | tf_op jit(solution)/shard_map/select_n | solution.py:135
  61.6 6.4 %fusion.31 = f32[1024]{0:T(1024)S(1)} fusion(pred[1024]{0:T(1024)(128)(4,1)S(1)} %get-tuple-element.205, pred[1024]{0:T(1024)(128)(4,1)S(1)} %get-tuple-element.204, pred[1024]{0:T(1024)(128)(4,1)S(1)} %get-tuple-element.203, pred[1024]{0:T(1024)(128)(4,1)S(1)} %get-tuple-element.202, pred[1024]{0:T(1024)(128)(4,1)S(1)} %get-tuple-element.201, ...), kind=kLoop, calls=%fused_computation.58 | loop fusion | flops 12288 | bytes 14376 | tf_op jit(solution)/shard_map/convert_element_type | solution.py:18
  68.0 6.3 %select_select_fusion = s32[1024]{0:T(1024)S(1)} fusion(pred[1024]{0:T(1024)(128)(4,1)S(1)} %get-tuple-element.205, pred[1024]{0:T(1024)(128)(4,1)S(1)} %get-tuple-element.204, pred[1024]{0:T(1024)(128)(4,1)S(1)} %get-tuple-element.203, pred[1024]{0:T(1024)(128)(4,1)S(1)} %get-tuple-element.202, pred[1024]{0:T(1024)(128)(4,1)S(1)} %get-tuple-element.201, ...), kind=kLoop, calls=%fused_computation.52 | loop fusion | flops 10240 | bytes 14376 | tf_op jit(solution)/shard_map/jit(_take)/select_n | solution.py:125
  74.3 42.7 %all_gather.28 = bf16[32,16,512]{2,1,0:T(8,128)(2,1)S(1)} all-gather(bf16[1,16,512]{2,1,0:T(8,128)(2,1)S(1)} %copy-done.4), channel_id=1, replica_groups=mesh['row'=8,'col'=32] {'col'}, dimensions={0}, use_global_device_ids=true | all-gather | bytes 540672 | tf_op jit(solution)/shard_map/all_gather | solution.py:117
  117.1 43.2 %all_gather.31 = bf16[32,16,256]{2,1,0:T(8,128)(2,1)} all-gather(bf16[1,16,256]{2,1,0:T(8,128)(2,1)S(1)} %copy-done.5), channel_id=1, replica_groups=mesh['row'=8,'col'=32] {'col'}, dimensions={0}, use_global_device_ids=true | all-gather | bytes 270336 | tf_op jit(solution)/shard_map/all_gather | solution.py:118
  160.3 1.0 multiply_cosine_fusion
  161.3 6.1 %fusion.40 = f32[1024,256]{0,1:T(8,128)S(1)} fusion(bf16[1024,4608]{0,1:T(8,128)(2,1)} %all-gather.6.cloned.1.call-done, bf16[4608,256]{1,0:T(8,128)(2,1)} %all-gather.12.cloned.1.call-done), kind=kOutput, calls=%fused_computation.91 | convolution fusion | flops 2415919104 | bytes 12845056 | tf_op jit(solution)/shard_map/dot_general | solution.py:106
  167.8 12.7 %copy.51 = bf16[1024,4608]{1,0:T(8,128)(2,1)} copy(bf16[1024,4608]{0,1:T(8,128)(2,1)} %all-gather.6.cloned.1.call-done) | data formatting | bytes 18874368
  180.6 9.1 %concatenate.11.clone = bf16[1216,4608]{1,0:T(8,128)(2,1)} pad(bf16[1024,4608]{1,0:T(8,128)(2,1)} %copy.51, bf16[]{:T(256)} %constant.127.clone.1), padding=0_192x0_0 | pad | bytes 20643842 | tf_op jit(solution)/shard_map/concatenate | solution.py:69
  189.6 6.1 %scatter_custom_fusion = bf16[2304,256]{1,0:T(8,128)(2,1)} fusion(s32[1024]{0:T(1024)S(1)} %get-tuple-element.195, bf16[1024,256]{1,0:T(8,128)(2,1)S(1)} %copy.49, bf16[]{:T(256)} %constant.127.clone.1), kind=kCustom, calls=%fused_computation.23 | custom fusion | bytes 1179650 | tf_op jit(solution)/shard_map/scatter | solution.py:135
  195.7 34.8 %all-gather.8.cloned.1.call-done = bf16[4608,512]{1,0:T(8,128)(2,1)} async-done(((bf16[144,512]{1,0:T(8,128)(2,1)}), bf16[4608,512]{1,0:T(8,128)(2,1)}) %all-gather.8.cloned.1.call-update) | async-done | bytes 4718608 | tf_op jit(solution)/shard_map/all_gather | solution.py:103
  230.6 9.1 %fusion.39 = f32[1024,512]{0,1:T(8,128)S(1)} fusion(bf16[1024,4608]{0,1:T(8,128)(2,1)} %all-gather.6.cloned.1.call-done, bf16[4608,512]{1,0:T(8,128)(2,1)} %all-gather.8.cloned.1.call-done), kind=kOutput, calls=%fused_computation.90 | convolution fusion | flops 4831838208 | bytes 16252928 | tf_op jit(solution)/shard_map/dot_general | solution.py:101
  239.7 97.2 %all-gather.10.cloned.1.call-done = bf16[32,4608,32]{1,2,0:T(8,128)(2,1)} async-done(((bf16[1,4608,32]{1,2,0:T(8,128)(2,1)}), bf16[32,4608,32]{1,2,0:T(8,128)(2,1)}) %all-gather.10.cloned.1.call-update) | async-done | bytes 9437200 | tf_op jit(solution)/shard_map/all_gather | solution.py:122
  336.9 91.2 %while.14 = (s32[]{:T(128)}, f32[1216,32]{0,1:T(8,128)S(1)}, s32[10]{0:T(128)S(1)}, bf16[1216,4608]{1,0:T(8,128)(2,1)}, s32[10]{0:T(128)S(1)}, /*index=5*/bf16[3...) while((s32[]{:T(128)}, f32[1216,32]{0,1:T(8,128)S(1)}, ...), condition=%wide.region_3.5_spmd.clone, body=%wide.region_2.4_spmd.clone.sunk | while | flops 56635784 | bytes 2165981 | solution.py:82
  343.2 2.2 fusion.52
  352.2 2.2 fusion.52
  361.3 2.2 fusion.52
  370.5 2.2 fusion.52
  379.6 2.2 fusion.52
  388.7 2.2 fusion.52
  397.9 2.2 fusion.52
  407.0 2.2 fusion.52
  416.2 2.2 fusion.52
  425.3 2.2 fusion.52
  428.1 0.8 bitcast_add_fusion
  429.4 1.3 copy.48
  431.3 7.0 %fusion.13 = bf16[1024,256]{1,0:T(8,128)(2,1)S(1)} fusion(f32[1024,256]{1,0:T(8,128)S(1)} %convolution_bitcast_fusion, bf16[1024,4608]{0,1:T(8,128)(2,1)} %all-gather.6.cloned.1.call-done, bf16[4608,256]{1,0:T(8,128)(2,1)} %all-gather.14.cloned.1.call-done), kind=kOutput, calls=%fused_computation.15 | convolution fusion | flops 2416443392 | bytes 13369344 | tf_op jit(solution)/shard_map/dot_general | solution.py:111
  438.3 6.1 %scatter_custom_fusion.1 = bf16[2304,256]{1,0:T(8,128)(2,1)} fusion(s32[1024]{0:T(1024)S(1)} %get-tuple-element.195, bf16[1024,256]{1,0:T(8,128)(2,1)S(1)} %fusion.13, bf16[]{:T(256)} %constant.127.clone.1), kind=kCustom, calls=%fused_computation.21 | custom fusion | bytes 1179650 | tf_op jit(solution)/shard_map/scatter | solution.py:141
  (102 shorter events, 37.4 us)
Async XLA Ops:
  7.2 27.6 %copy-start = (s32[32]{0:T(128)S(1)}, s32[32]{0:T(128)}, u32[]{:S(2)}) copy-start(s32[32]{0:T(128)} %param.24) | copy-start | bytes 388
  7.2 154.1 %all-gather.12.cloned.1.call-start = ((), (), s32[]{:S(2)}) async-start(), calls=%async_computation.3 | async-start | bytes 2433024 | tf_op jit(solution)/shard_map/all_gather | solution.py:108
  7.9 153.4 %all-gather.6.cloned.1.call-start = ((), (), s32[]{:S(2)}) async-start(), calls=%async_computation | async-start | bytes 10616832 | tf_op jit(solution)/shard_map/all_gather | solution.py:100
  8.7 221.9 %all-gather.8.cloned.1.call-start = ((), (), s32[]{:S(2)}) async-start(), calls=%async_computation.1 | async-start | bytes 4866048 | tf_op jit(solution)/shard_map/all_gather | solution.py:103
  9.4 327.5 %all-gather.10.cloned.1.call-start = ((), (), s32[]{:S(2)}) async-start(), calls=%async_computation.2 | async-start | bytes 9732096 | tf_op jit(solution)/shard_map/all_gather | solution.py:122
  10.4 23.2 %copy-start.3 = (s32[1,18]{1,0:T(1,128)S(1)}, s32[1,18]{1,0:T(1,128)}, u32[]{:S(2)}) copy-start(s32[1,18]{1,0:T(1,128)} %param.25) | copy-start | bytes 220
  10.4 23.9 %copy-start.7 = (s32[1,10]{1,0:T(1,128)S(1)}, s32[1,10]{1,0:T(1,128)}, u32[]{:S(2)}) copy-start(s32[1,10]{1,0:T(1,128)} %param.22) | copy-start | bytes 124
  10.4 24.1 %copy-start.6 = (s32[1,10]{1,0:T(1,128)S(1)}, s32[1,10]{1,0:T(1,128)}, u32[]{:S(2)}) copy-start(s32[1,10]{1,0:T(1,128)} %param.23) | copy-start | bytes 124
  29.3 45.1 %copy-start.4 = (bf16[1,16,512]{2,1,0:T(8,128)(2,1)S(1)}, bf16[1,16,512]{2,1,0:T(8,128)(2,1)}, u32[]{:S(2)}) copy-start(bf16[1,16,512]{2,1,0:T(8,128)(2,1)} %param.20) | copy-start | bytes 49156
  29.3 87.8 %copy-start.5 = (bf16[1,16,256]{2,1,0:T(8,128)(2,1)S(1)}, bf16[1,16,256]{2,1,0:T(8,128)(2,1)}, u32[]{:S(2)}) copy-start(bf16[1,16,256]{2,1,0:T(8,128)(2,1)} %param.21) | copy-start | bytes 24580
  33.0 398.3 %all-gather.14.cloned.1.call-start = ((), (), s32[]{:S(2)}) async-start(), calls=%async_computation.4 | async-start | bytes 2433024 | tf_op jit(solution)/shard_map/all_gather | solution.py:113
  429.3 1.4 copy-start.2
  431.3 13.1 %copy-start.1 = (s32[32]{0:T(128)S(1)}, s32[32]{0:T(128)}, u32[]{:S(2)}) copy-start(s32[32]{0:T(128)} %param.24) | copy-start | bytes 388
Sparse Core Ops, SparseCore 0:
  10.6 77.8 all-gather.11
  90.3 58.5 all-gather.5
  151.5 79.0 all-gather.7
  233.6 103.2 all-gather.9
  339.3 71.4 all-gather.13
where the time goes:
time: 453 us; the launch traced here: 451 us
  waiting for transfers between devices  135 us (30%)
  blocking collectives  105 us (23%)
  local copies, waits for them, and re-layouts  67.1 us (15%)
  matrix products  45.5 us (10%)
  other arithmetic  45.3 us (10%)
  loops' own time  39.3 us (9%)
  between operations  14.1 us (3%)
    all_gather x1, waiting for transfers between devices, shards(): down_all = lax.all_gather(rows_all, 'col', axis=0, tiled=True)  97.2 us
    all_gather x1, blocking collectives, shards(): lax.all_gather(adapter_up_value, 'col', axis=0, tiled=True)  43.2 us
    all_gather x1, blocking collectives, shards(): lax.all_gather(adapter_up_query, 'col', axis=0, tiled=True)  42.7 us
    another operation x1, loops' own time, project_down(): result = lax.fori_loop(0, starts.shape[0], one_request, result)  39.3 us
    all_gather x1, waiting for transfers between devices, shards(): lax.all_gather(w_query, 'col', axis=0, tiled=True)  34.8 us
    select_n x1, other arithmetic, shards(): key_cache = jnp.zeros((pages * PAGE, key_width), jnp.bfloat16).at[target]...  24 us
    dot_general x10, matrix products, one_request(): partial_sum = jnp.dot(window, factor, preferred_element_type=jnp.float32)  22 us
    all_gather x1, blocking collectives, shards(): rows_all = lax.all_gather(adapter_down, 'row', axis=1, tiled=True)  18.8 us
  transfers between devices with their start and end apart: 5, of which 2 were waited for; matrix products, arithmetic and copies ran while one was open for 32% of the time, Pallas kernels for 0%

commit v1 on v0

--- a/solution.py
+++ b/solution.py
@@ -8,6 +8,27 @@
 PAGE = 128
 MOST = 192
 TOK_DEV = 1024
+
+
+def collect(shard, axis, dim):
+    length, here, extent = (lax.axis_size(axis), lax.axis_index(axis), shard.shape[dim])
+    upward = [(i, (i + 1) % length) for i in range(length)]
+    left = [(i, (i - 1) % length) for i in range(length)]
+    out = jnp.zeros((*shard.shape[:dim], length * extent, *shard.shape[dim + 1 :]), shard.dtype)
+    out = lax.dynamic_update_slice_in_dim(out, shard, here * extent, axis=dim)
+    from_left = from_right = shard
+    halfway = length // 2
+    for step in range(1, halfway + 1):
+        from_left = lax.ppermute(from_left, axis, upward)
+        out = lax.dynamic_update_slice_in_dim(
+            out, from_left, (here - step) % length * extent, axis=dim
+        )
+        if step < length - halfway:
+            from_right = lax.ppermute(from_right, axis, left)
+            out = lax.dynamic_update_slice_in_dim(
+                out, from_right, (here + step) % length * extent, axis=dim
+            )
+    return out
 
 
 def rotate(values, position):
@@ -118,7 +139,7 @@
         lax.all_gather(adapter_up_value, "col", axis=0, tiled=True),
     )
     chosen_request = jnp.take(adapter_slot, request_adapter[0])
-    rows_all = lax.all_gather(adapter_down, "row", axis=1, tiled=True)
+    rows_all = collect(adapter_down, "row", 1)
     down_all = lax.all_gather(rows_all, "col", axis=0, tiled=True)
     lowrank = project_down(full_rows, down_all, starts, lengths[0], chosen_request)
     lowrank = lowrank.astype(jnp.bfloat16)

time: 453 us -> 453 us (level)
  blocking collectives: 105 us -> 86.8 us
  starting transfers between devices: 0.19 us -> 11.4 us
  waiting for transfers between devices: 135 us -> 140 us
    all_gather x1 -> x0, blocking collectives: 18.8 us -> none  [shards(): rows_all = lax.all_gather(adapter_down, 'row', axis=1, tiled=True)]
    ppermute x0 -> x7, starting transfers between devices: none -> 11.2 us  [the longest x4 5.85 us: collect(): from_left = lax.ppermute(from_left, axis, upward)]
    dynamic_update_slice x0 -> x8, local copies, waits for them, and re-layouts: none -> 5.24 us  [the longest x4 2.22 us: collect(): lax.dynamic_update_slice_in_dim(out, from_left, (here - step) % length *...]
    unnamed x18 -> x17, local copies, waits for them, and re-layouts: 13.7 us -> 13.5 us
  transfers between devices with their start and end apart: 5 -> 12, of which waited for: 2 -> 5; matrix products, arithmetic and copies ran while one was open for 32% -> 32% of each run, Pallas kernels for 0% -> 0%
where the time goes in v1:
time: 453 us; the launch traced here: 451 us
  waiting for transfers between devices  140 us (31%)
  blocking collectives  86.8 us (19%)
  local copies, waits for them, and re-layouts  68.6 us (15%)
  matrix products  45.5 us (10%)
  other arithmetic  45.4 us (10%)
  loops' own time  39.3 us (9%)
  between operations  14.2 us (3%)
  starting transfers between devices  11.4 us (3%)
    all_gather x1, waiting for transfers between devices, shards(): down_all = lax.all_gather(rows_all, 'col', axis=0, tiled=True)  97.2 us
    all_gather x1, blocking collectives, shards(): lax.all_gather(adapter_up_query, 'col', axis=0, tiled=True)  44.3 us
    all_gather x1, blocking collectives, shards(): lax.all_gather(adapter_up_value, 'col', axis=0, tiled=True)  42.5 us
    another operation x1, loops' own time, project_down(): result = lax.fori_loop(0, starts.shape[0], one_request, result)  39.3 us
    all_gather x1, waiting for transfers between devices, shards(): lax.all_gather(w_query, 'col', axis=0, tiled=True)  37.9 us
    select_n x1, other arithmetic, shards(): key_cache = jnp.zeros((pages * PAGE, key_width), jnp.bfloat16).at[target]...  24.2 us
    dot_general x10, matrix products, one_request(): partial_sum = jnp.dot(window, factor, preferred_element_type=jnp.float32)  22 us
    unnamed x17, local copies, waits for them, and re-layouts  13.5 us
  transfers between devices with their start and end apart: 12, of which 5 were waited for; matrix products, arithmetic and copies ran while one was open for 32% of the time, Pallas kernels for 0%

profile of v1, /device:TPU:1, one launch (start us, length us, event | category | flops | bytes accessed | tf_op | source)
XLA Modules:
  0.0 451.1 jit_solution(13747035122756696652)
XLA Ops:
  9.5 2.7 collective-permute-start
  13.6 2.2 collective-permute-start.2
  15.8 1.8 collective-permute-start.3
  19.3 3.0 collective-permute-start.5
  22.9 1.3 dynamic_update_slice.31
  29.7 44.3 %all_gather.24 = bf16[32,16,512]{2,1,0:T(8,128)(2,1)S(1)} all-gather(bf16[1,16,512]{2,1,0:T(8,128)(2,1)S(1)} %copy-done.4), channel_id=1, replica_groups=mesh['row'=8,'col'=32] {'col'}, dimensions={0}, use_global_device_ids=true | all-gather | bytes 540672 | tf_op jit(solution)/shard_map/all_gather | solution.py:138
  78.0 24.2 %compare_select_fusion.1 = (s32[1024]{0:T(1024)S(1)}, pred[1024]{0:T(1024)(128)(4,1)S(1)}, pred[1024]{0:T(1024)(128)(4,1)S(1)}, pred[1024]{0:T(1024)(128)(4,1)S(...) fusion(s32[]{:T(128)} %bitcast.41, s32[]{:T(128)} %bitcast.40, ...), kind=kLoop, calls=%fused_computation.41 | loop fusion | flops 105472 | bytes 18584 | tf_op jit(solution)/shard_map/select_n | solution.py:156
  102.3 6.4 %fusion.31 = f32[1024]{0:T(1024)S(1)} fusion(pred[1024]{0:T(1024)(128)(4,1)S(1)} %get-tuple-element.198, pred[1024]{0:T(1024)(128)(4,1)S(1)} %get-tuple-element.197, pred[1024]{0:T(1024)(128)(4,1)S(1)} %get-tuple-element.196, pred[1024]{0:T(1024)(128)(4,1)S(1)} %get-tuple-element.195, pred[1024]{0:T(1024)(128)(4,1)S(1)} %get-tuple-element.194, ...), kind=kLoop, calls=%fused_computation.58 | loop fusion | flops 12288 | bytes 14376 | tf_op jit(solution)/shard_map/convert_element_type | solution.py:39
  108.7 6.1 %select_select_fusion = s32[1024]{0:T(1024)S(1)} fusion(pred[1024]{0:T(1024)(128)(4,1)S(1)} %get-tuple-element.198, pred[1024]{0:T(1024)(128)(4,1)S(1)} %get-tuple-element.197, pred[1024]{0:T(1024)(128)(4,1)S(1)} %get-tuple-element.196, pred[1024]{0:T(1024)(128)(4,1)S(1)} %get-tuple-element.195, pred[1024]{0:T(1024)(128)(4,1)S(1)} %get-tuple-element.194, ...), kind=kLoop, calls=%fused_computation.52 | loop fusion | flops 10240 | bytes 14376 | tf_op jit(solution)/shard_map/jit(_take)/select_n | solution.py:146
  114.9 42.5 %all_gather.27 = bf16[32,16,256]{2,1,0:T(8,128)(2,1)} all-gather(bf16[1,16,256]{2,1,0:T(8,128)(2,1)S(1)} %copy-done.5), channel_id=1, replica_groups=mesh['row'=8,'col'=32] {'col'}, dimensions={0}, use_global_device_ids=true | all-gather | bytes 270336 | tf_op jit(solution)/shard_map/all_gather | solution.py:139
  157.4 1.0 multiply_cosine_fusion
  158.4 12.8 %copy.45 = bf16[1024,4608]{1,0:T(8,128)(2,1)} copy(bf16[1024,4608]{0,1:T(8,128)(2,1)} %all-gather.6.cloned.1.call-done) | data formatting | bytes 18874368
  171.2 9.2 %concatenate.11.clone = bf16[1216,4608]{1,0:T(8,128)(2,1)} pad(bf16[1024,4608]{1,0:T(8,128)(2,1)} %copy.45, bf16[]{:T(256)} %constant.176.clone.1), padding=0_192x0_0 | pad | bytes 20643842 | tf_op jit(solution)/shard_map/concatenate | solution.py:90
  180.4 6.0 %fusion.40 = f32[1024,256]{0,1:T(8,128)S(1)} fusion(bf16[1024,4608]{0,1:T(8,128)(2,1)} %all-gather.6.cloned.1.call-done, bf16[4608,256]{1,0:T(8,128)(2,1)} %all-gather.12.cloned.1.call-done), kind=kOutput, calls=%fused_computation.91 | convolution fusion | flops 2415919104 | bytes 12845056 | tf_op jit(solution)/shard_map/dot_general | solution.py:127
  186.8 6.1 %scatter_custom_fusion = bf16[2304,256]{1,0:T(8,128)(2,1)} fusion(s32[1024]{0:T(1024)S(1)} %get-tuple-element.188, bf16[1024,256]{1,0:T(8,128)(2,1)S(1)} %copy.43, bf16[]{:T(256)} %constant.176.clone.1), kind=kCustom, calls=%fused_computation.23 | custom fusion | bytes 1179650 | tf_op jit(solution)/shard_map/scatter | solution.py:156
  192.9 37.9 %all-gather.8.cloned.1.call-done = bf16[4608,512]{1,0:T(8,128)(2,1)} async-done(((bf16[144,512]{1,0:T(8,128)(2,1)}), bf16[4608,512]{1,0:T(8,128)(2,1)}) %all-gather.8.cloned.1.call-update) | async-done | bytes 4718608 | tf_op jit(solution)/shard_map/all_gather | solution.py:124
  230.7 9.1 %fusion.39 = f32[1024,512]{0,1:T(8,128)S(1)} fusion(bf16[1024,4608]{0,1:T(8,128)(2,1)} %all-gather.6.cloned.1.call-done, bf16[4608,512]{1,0:T(8,128)(2,1)} %all-gather.8.cloned.1.call-done), kind=kOutput, calls=%fused_computation.90 | convolution fusion | flops 4831838208 | bytes 16252928 | tf_op jit(solution)/shard_map/dot_general | solution.py:122
  239.8 97.2 %all-gather.10.cloned.1.call-done = bf16[32,4608,32]{1,2,0:T(8,128)(2,1)} async-done(((bf16[1,4608,32]{1,2,0:T(8,128)(2,1)}), bf16[32,4608,32]{1,2,0:T(8,128)(2,1)}) %all-gather.10.cloned.1.call-update) | async-done | bytes 9437200 | tf_op jit(solution)/shard_map/all_gather | solution.py:143
  337.1 91.2 %while.14 = (s32[]{:T(128)}, f32[1216,32]{0,1:T(8,128)S(1)}, s32[10]{0:T(128)S(1)}, bf16[1216,4608]{1,0:T(8,128)(2,1)}, s32[10]{0:T(128)S(1)}, /*index=5*/bf16[3...) while((s32[]{:T(128)}, f32[1216,32]{0,1:T(8,128)S(1)}, ...), condition=%wide.region_3.5_spmd.clone, body=%wide.region_2.4_spmd.clone.sunk | while | flops 56635784 | bytes 2165989 | solution.py:103
  343.4 2.2 fusion.52
  352.4 2.2 fusion.52
  361.5 2.2 fusion.52
  370.6 2.2 fusion.52
  379.8 2.2 fusion.52
  388.9 2.2 fusion.52
  398.0 2.2 fusion.52
  407.2 2.2 fusion.52
  416.3 2.2 fusion.52
  425.5 2.2 fusion.52
  429.6 1.3 copy.42
  431.4 7.0 %fusion.13 = bf16[1024,256]{1,0:T(8,128)(2,1)S(1)} fusion(f32[1024,256]{1,0:T(8,128)S(1)} %convolution_bitcast_fusion, bf16[1024,4608]{0,1:T(8,128)(2,1)} %all-gather.6.cloned.1.call-done, bf16[4608,256]{1,0:T(8,128)(2,1)} %all-gather.14.cloned.1.call-done), kind=kOutput, calls=%fused_computation.15 | convolution fusion | flops 2416443392 | bytes 13369344 | tf_op jit(solution)/shard_map/dot_general | solution.py:132
  438.5 6.1 %scatter_custom_fusion.1 = bf16[2304,256]{1,0:T(8,128)(2,1)} fusion(s32[1024]{0:T(1024)S(1)} %get-tuple-element.188, bf16[1024,256]{1,0:T(8,128)(2,1)S(1)} %fusion.13, bf16[]{:T(256)} %constant.176.clone.1), kind=kCustom, calls=%fused_computation.21 | custom fusion | bytes 1179650 | tf_op jit(solution)/shard_map/scatter | solution.py:162
  (123 shorter events, 47.4 us)
Async XLA Ops:
  7.2 67.3 %copy-start = (s32[32]{0:T(128)S(1)}, s32[32]{0:T(128)}, u32[]{:S(2)}) copy-start(s32[32]{0:T(128)} %param.24) | copy-start | bytes 388
  7.2 22.5 %copy-start.4 = (bf16[1,16,512]{2,1,0:T(8,128)(2,1)S(1)}, bf16[1,16,512]{2,1,0:T(8,128)(2,1)}, u32[]{:S(2)}) copy-start(bf16[1,16,512]{2,1,0:T(8,128)(2,1)} %param.20) | copy-start | bytes 49156
  7.2 66.8 %copy-start.6 = (s32[1,10]{1,0:T(1,128)S(1)}, s32[1,10]{1,0:T(1,128)}, u32[]{:S(2)}) copy-start(s32[1,10]{1,0:T(1,128)} %param.22) | copy-start | bytes 124
  7.2 67.2 %copy-start.7 = (s32[1,10]{1,0:T(1,128)S(1)}, s32[1,10]{1,0:T(1,128)}, u32[]{:S(2)}) copy-start(s32[1,10]{1,0:T(1,128)} %param.23) | copy-start | bytes 124
  7.2 69.3 %copy-start.3 = (s32[1,18]{1,0:T(1,128)S(1)}, s32[1,18]{1,0:T(1,128)}, u32[]{:S(2)}) copy-start(s32[1,18]{1,0:T(1,128)} %param.25) | copy-start | bytes 220
  7.2 107.6 %copy-start.5 = (bf16[1,16,256]{2,1,0:T(8,128)(2,1)S(1)}, bf16[1,16,256]{2,1,0:T(8,128)(2,1)}, u32[]{:S(2)}) copy-start(bf16[1,16,256]{2,1,0:T(8,128)(2,1)} %param.21) | copy-start | bytes 24580
  7.2 151.1 %all-gather.6.cloned.1.call-start = ((), (), s32[]{:S(2)}) async-start(), calls=%async_computation | async-start | bytes 10616832 | tf_op jit(solution)/shard_map/all_gather | solution.py:121
  8.0 172.4 %all-gather.12.cloned.1.call-start = ((), (), s32[]{:S(2)}) async-start(), calls=%async_computation.3 | async-start | bytes 2433024 | tf_op jit(solution)/shard_map/all_gather | solution.py:129
  8.7 222.0 %all-gather.8.cloned.1.call-start = ((), (), s32[]{:S(2)}) async-start(), calls=%async_computation.1 | async-start | bytes 4866048 | tf_op jit(solution)/shard_map/all_gather | solution.py:124
  9.4 327.6 %all-gather.10.cloned.1.call-start = ((), (), s32[]{:S(2)}) async-start(), calls=%async_computation.2 | async-start | bytes 9732096 | tf_op jit(solution)/shard_map/all_gather | solution.py:143
  9.5 4.1 collective-permute-start
  12.2 3.6 collective-permute-start.1
  13.6 4.6 %collective-permute-start.2 = (bf16[1,576,32]{1,2,0:T(8,128)(2,1)S(1)}, bf16[1,576,32]{1,2,0:T(8,128)(2,1)S(1)}, u32[]{:S(2)}, u32[]{:S(2)}) collective-permute-start(bf16[1,576,32]{1,2,0:T(8,128)(2,1)S(1)} %collective-permute-done), channel_id=1, source_target_pairs={{0,32},{32,64},{64,96},{96,128},{128,160},{160,192},{192,224},{224... | collective-permute-start | bytes 110600 | tf_op jit(solution)/shard_map/ppermute | solution.py:22
  15.8 3.4 collective-permute-start.3
  18.3 4.6 %collective-permute-start.4 = (bf16[1,576,32]{1,2,0:T(8,128)(2,1)S(1)}, bf16[1,576,32]{1,2,0:T(8,128)(2,1)S(1)}, u32[]{:S(2)}, u32[]{:S(2)}) collective-permute-start(bf16[1,576,32]{1,2,0:T(8,128)(2,1)S(1)} %collective-permute-done.2), channel_id=1, source_target_pairs={{0,32},{32,64},{64,96},{96,128},{128,160},{160,192},{192,224},{224... | collective-permute-start | bytes 110600 | tf_op jit(solution)/shard_map/ppermute | solution.py:22
  19.3 7.8 %collective-permute-start.5 = (bf16[1,576,32]{1,2,0:T(8,128)(2,1)S(1)}, bf16[1,576,32]{1,2,0:T(8,128)(2,1)S(1)}, u32[]{:S(2)}, u32[]{:S(2)}) collective-permute-start(bf16[1,576,32]{1,2,0:T(8,128)(2,1)S(1)} %collective-permute-done.3), channel_id=1, source_target_pairs={{0,224},{32,0},{64,32},{96,64},{128,96},{160,128},{192,160},{224,1... | collective-permute-start | bytes 110600 | tf_op jit(solution)/shard_map/ppermute | solution.py:27
  22.9 4.7 %collective-permute-start.6 = (bf16[1,576,32]{1,2,0:T(8,128)(2,1)S(1)}, bf16[1,576,32]{1,2,0:T(8,128)(2,1)S(1)}, u32[]{:S(2)}, u32[]{:S(2)}) collective-permute-start(bf16[1,576,32]{1,2,0:T(8,128)(2,1)S(1)} %collective-permute-done.4), channel_id=1, source_target_pairs={{0,32},{32,64},{64,96},{96,128},{128,160},{160,192},{192,224},{224... | collective-permute-start | bytes 110600 | tf_op jit(solution)/shard_map/ppermute | solution.py:22
  28.3 0.7 copy-start.1
  29.0 402.4 %all-gather.14.cloned.1.call-start = ((), (), s32[]{:S(2)}) async-start(), calls=%async_computation.4 | async-start | bytes 2433024 | tf_op jit(solution)/shard_map/all_gather | solution.py:134
  429.5 1.4 copy-start.2
Sparse Core Ops, SparseCore 0:
  9.9 61.0 all-gather.5
  73.6 73.6 all-gather.11
  149.9 80.8 all-gather.7
  233.8 103.2 all-gather.9
  339.5 71.4 all-gather.13
